TPU v7x, 256 devices: a whole 4x4x8 slice. The times are simulated.
256 devices in a mesh: sample: 32 (over x, y, core), slab: 8 (over z).
Axes of the slice: x: 4, y: 4, z: 8, core: 2. Of those that a mesh axis runs over, the one named last changes fastest.
Arguments:
- volume: bfloat16 [4, 32, 32, 4096], P(None, 'sample', 'slab'), may hold values from -6 to 6
- cotangent: bfloat16 [128, 32, 8, 256], P(None, 'sample', 'slab'), may hold values from -0.5 to 0.5
- w_first: bfloat16 [27, 4, 32], replicated, may hold values from -0.625 to 0.625
- b_first: float32 [32], replicated, may hold values from -3 to 3
- w_second: bfloat16 [27, 32, 64], replicated, may hold values from -0.21875 to 0.21875
- b_second: float32 [64], replicated, may hold values from -3 to 3
- w_third: bfloat16 [27, 64, 128], replicated, may hold values from -0.15625 to 0.15625
- b_third: float32 [128], replicated, may hold values from -3 to 3
Outputs:
- features: bfloat16 [128, 32, 8, 256], P(None, 'sample', 'slab')
- kernel_grad_first: float32 [27, 4, 32], replicated
- bias_grad_first: float32 [32], replicated
- kernel_grad_second: float32 [27, 32, 64], replicated
- bias_grad_second: float32 [64], replicated
- kernel_grad_third: float32 [27, 64, 128], replicated
- bias_grad_third: float32 [128], replicated
All inputs are finite; a program needn't handle non-finite values.
Results may differ from a plain program's by a relative error of at most 0.02.
Values may be sent and summed in bfloat16 or wider, within the bound.
No kernel may reach another device: no remote copies, remote signals or barrier semaphores. Data moves between devices by JAX's collectives and lax.ppermute only.
A program may use at most 128 MiB of HBM per device.

v0:
```python
import jax
import jax.numpy as jnp
from jax import lax
from jax.sharding import PartitionSpec as P

SX = 32
CZ = 4


def with_halo(shard, sides, width):
    for axis, dim in sides:
        size, length = (lax.axis_size(axis), shard.shape[dim])
        up = [(i, (i + 1) % size) for i in range(size - 1)]
        down = [(j, i) for i, j in up]
        last = lax.slice_in_dim(shard, length - width, length, axis=dim)
        first = lax.slice_in_dim(shard, 0, width, axis=dim)
        before = lax.ppermute(last, axis, up)
        after = lax.ppermute(first, axis, down)
        shard = jnp.concatenate([before, shard, after], axis=dim)
    return shard


def silu_slope(values):
    sigmoid = jax.nn.sigmoid(values)
    return sigmoid * (1.0 + values * (1.0 - sigmoid))


def put_block(values, update, sample, depth_start):
    return lax.dynamic_update_slice(values, update, (0, sample, depth_start, 0))


def gather_taps(section, row_width):
    depth_len = section.shape[2] - 2
    plane_size = section.shape[3]
    flattened = jnp.pad(section, ((0, 0), (0, 0), (0, 0), (row_width + 1, row_width + 1)))
    column = lax.broadcasted_iota(jnp.int32, (1, 1, 1, plane_size), 3) % row_width
    left_mask = (column >= 1).astype(section.dtype)
    right_mask = (column <= row_width - 2).astype(section.dtype)
    pieces = []
    for tap_index in range(27):
        depth_start = tap_index // 9
        row_step = tap_index // 3 % 3 - 1
        col_step = tap_index % 3 - 1
        offset = row_width + 1 + row_step * row_width + col_step
        shifted = flattened[
            :, :, depth_start : depth_start + depth_len, offset : offset + plane_size
        ]
        if col_step < 0:
            shifted = shifted * left_mask
        elif col_step > 0:
            shifted = shifted * right_mask
        pieces.append(shifted)
    return jnp.concatenate(pieces, axis=0)


def apply_weight(patches, weight):
    flat_weight = weight.reshape(weight.shape[0] * weight.shape[1], weight.shape[2])
    return jnp.einsum("ko,kgzp->ogzp", flat_weight, patches, preferred_element_type=jnp.float32)


def weight_term(patches, grad_block, in_channels):
    summed = jnp.einsum("kgzp,ogzp->ko", patches, grad_block, preferred_element_type=jnp.float32)
    return summed.reshape(27, in_channels, grad_block.shape[0])


def pool_cells(values, row_width):
    channels, samples, depth_len, plane_size = values.shape
    row_count = plane_size // row_width
    grouped = values.reshape(
        channels, samples, depth_len // 2, 2, row_count // 2, 2, row_width // 2, 2
    )
    return grouped.mean(axis=(3, 5, 7)).reshape(channels, samples, depth_len // 2, plane_size // 4)


def spread_cells(values, coarse_width):
    channels, samples, depth_len, plane_size = values.shape
    row_count = plane_size // coarse_width
    grouped = values.reshape(channels, samples, depth_len, 1, row_count, 1, coarse_width, 1)
    grouped = jnp.broadcast_to(
        grouped, (channels, samples, depth_len, 2, row_count, 2, coarse_width, 2)
    )
    return grouped.reshape(channels, samples, 2 * depth_len, 4 * plane_size) * 0.125


def forward_layer(padded, weight, bias_values, row_width, depth_block, pooled_out):
    out_channels = weight.shape[2]
    samples, depth_total, plane_size = (padded.shape[1], padded.shape[2] - 2, padded.shape[3])
    per_sample = depth_total // depth_block
    pre_buffer = jnp.zeros((out_channels, samples, depth_total, plane_size), jnp.bfloat16)
    if pooled_out:
        out_buffer = jnp.zeros(
            (out_channels, samples, depth_total // 2, plane_size // 4), jnp.bfloat16
        )
    else:
        out_buffer = jnp.zeros_like(pre_buffer)

    def forward_block_step(block_index, buffers):
        sample = block_index // per_sample
        depth_start = block_index % per_sample * depth_block
        pre_values = (
            apply_weight(gather_taps(padded, row_width), weight) + bias_values[:, None, None, None]
        ).astype(jnp.bfloat16)
        activated = jax.nn.silu(pre_values.astype(jnp.float32))
        if pooled_out:
            result = put_block(
                buffers[1],
                pool_cells(activated, row_width).astype(jnp.bfloat16),
                sample,
                depth_start // 2,
            )
        else:
            result = put_block(buffers[1], activated.astype(jnp.bfloat16), sample, depth_start)
        return (put_block(buffers[0], pre_values, sample, depth_start), result)

    return lax.fori_loop(0, samples * per_sample, forward_block_step, (pre_buffer, out_buffer))


def weight_grads(padded, delta_values, row_width, depth_block, weight):
    samples, depth_total = (delta_values.shape[1], delta_values.shape[2])
    per_sample = depth_total // depth_block
    in_channels = weight.shape[1]

    def weight_block_step(block_index, summed):
        return summed + weight_term(gather_taps(padded, row_width), delta_values, in_channels)

    return lax.fori_loop(
        0, samples * per_sample, weight_block_step, jnp.zeros(weight.shape, jnp.float32)
    )


def data_grads(padded, flipped, row_width, depth_block):
    out_channels = flipped.shape[2]
    samples, depth_total, plane_size = (padded.shape[1], padded.shape[2] - 2, padded.shape[3])
    per_sample = depth_total // depth_block
    out_buffer = jnp.zeros((out_channels, samples, depth_total, plane_size), jnp.bfloat16)

    def data_block_step(block_index, buffer_now):
        sample = block_index // per_sample
        depth_start = block_index % per_sample * depth_block
        result = apply_weight(gather_taps(padded, row_width), flipped).astype(jnp.bfloat16)
        return put_block(buffer_now, result, sample, depth_start)

    return lax.fori_loop(0, samples * per_sample, data_block_step, out_buffer)


def bias_sum(delta_values):
    return jnp.sum(delta_values, axis=(1, 2, 3), dtype=jnp.float32)


def per_device(volume, cotangent, w_first, b_first, w_second, b_second, w_third, b_third):
    flipped_second = jnp.flip(w_second, 0).transpose(0, 2, 1)
    flipped_third = jnp.flip(w_third, 0).transpose(0, 2, 1)
    volume_padded = with_halo(volume, (("slab", 2),), 1)
    first_pre, first_pooled = forward_layer(volume_padded, w_first, b_first, SX, CZ, True)
    first_padded = with_halo(first_pooled, (("slab", 2),), 1)
    second_pre, second_pooled = forward_layer(
        first_padded, w_second, b_second, SX // 2, CZ // 2, True
    )
    coarse_depth = second_pooled.shape[2]
    third_padded = with_halo(second_pooled, (("slab", 2),), 1)
    third_pre, features = forward_layer(
        third_padded, w_third, b_third, SX // 4, coarse_depth, False
    )
    third_delta = (
        cotangent.astype(jnp.float32) * silu_slope(third_pre.astype(jnp.float32))
    ).astype(jnp.bfloat16)
    kernel_third = weight_grads(third_padded, third_delta, SX // 4, coarse_depth, w_third)
    bias_third = bias_sum(third_delta)
    kernel_third, bias_third = lax.psum((kernel_third, bias_third), ("sample", "slab"))
    delta_window = with_halo(third_delta, (("slab", 2),), 1)
    second_back = data_grads(delta_window, flipped_third, SX // 4, coarse_depth)
    second_delta = (
        spread_cells(second_back.astype(jnp.float32), SX // 4)
        * silu_slope(second_pre.astype(jnp.float32))
    ).astype(jnp.bfloat16)
    kernel_second = weight_grads(first_padded, second_delta, SX // 2, CZ // 2, w_second)
    bias_second = bias_sum(second_delta)
    delta_padded = with_halo(second_delta, (("slab", 2),), 1)
    first_back = data_grads(delta_padded, flipped_second, SX // 2, CZ // 2)
    first_delta = (
        spread_cells(first_back.astype(jnp.float32), SX // 2)
        * silu_slope(first_pre.astype(jnp.float32))
    ).astype(jnp.bfloat16)
    kernel_first = weight_grads(volume_padded, first_delta, SX, CZ, w_first)
    bias_first = bias_sum(first_delta)
    kernel_first, bias_first, kernel_second, bias_second = lax.psum(
        (kernel_first, bias_first, kernel_second, bias_second), ("sample", "slab")
    )
    return (
        features,
        kernel_first,
        bias_first,
        kernel_second,
        bias_second,
        kernel_third,
        bias_third,
    )


def solution(mesh):
    in_specs = (
        P(None, "sample", "slab", None),
        P(None, "sample", "slab", None),
        P(),
        P(),
        P(),
        P(),
        P(),
        P(),
    )
    out_specs = (P(None, "sample", "slab", None), P(), P(), P(), P(), P(), P())
    return jax.shard_map(
        per_device, mesh=mesh, in_specs=in_specs, out_specs=out_specs, check_vma=False
    )
```

profile of v0, /device:TPU:1, one launch (start us, length us, event | category | flops | bytes accessed | tf_op | source)
XLA Modules:
  0.0 395.6 jit_solution(9042423092520511804)
XLA Ops:
  7.2 1.0 copy.58
  8.3 4.4 %collective-permute-start = (bf16[4,1,1,4096]{3,0,2,1:T(4,128)(2,1)S(1)}, bf16[4,1,1,4096]{3,0,2,1:T(4,128)(2,1)S(1)}, u32[]{:S(2)}, u32[]{:S(2)}) collective-permute-start(bf16[4,1,1,4096]{3,0,2,1:T(4,128)(2,1)S(1)} %get-tuple-element.223), channel_id=1, source_target_pairs={{0,1},{1,2},{2,3},{3,4},{4,5},{5,6},{6,7},{8,9},{9,10},{10,11},{11... | collective-permute-start | bytes 98312 | tf_op jit(solution)/shard_map/ppermute | solution.py:17
  12.6 1.3 collective-permute-start.1
  14.0 0.6 fusion.115
  14.6 0.9 reverse_bitcast_fusion.1
  15.5 1.0 reverse_bitcast_fusion
  16.6 1.4 reshape.324
  18.0 0.6 copy-done.3
  18.6 0.6 copy-done.5
  19.4 1.3 slice_multiply_fusion.36
  20.7 1.7 slice_multiply_fusion.37
  22.4 16.2 %concatenate.62 = bf16[108,1,4,4096]{3,0,2,1:T(8,128)(2,1)} concatenate(bf16[4,1,4,4096]{3,0,2,1:T(4,128)(2,1)} %get-tuple-element.212, bf16[4,1,4,4096]{3,0,2,1:T(4,128)(2,1)S(1)} %get-tuple-element.218, bf16[4,1,4,4096]{3,0,2,1:T(4,128)(2,1)S(1)} %get-tuple-element.203, bf16[4,1,4,4096]{3,0,2,1:T(4,128)(2,1)} %get-tuple-element.211, ...), dimensions={0} | concatenate | bytes 7077888 | tf_op jit(solution)/shard_map/while/body/eval_jaxpr/concatenate | solution.py:53
  38.6 4.7 %fusion.10 = (f32[32,4,4096]{2,0,1:T(8,128)S(1)}, f32[32,4,4096]{2,0,1:T(8,128)}) fusion(f32[32]{0:T(128)} %param.11, bf16[108,32]{1,0:T(8,128)(2,1)} %reshape.324, bf16[108,1,4,4096]{3,0,2,1:T(8,128)(2,1)} %concatenate.62), kind=kOutput, calls=%fused_computation.14 | convolution fusion | flops 116916224 | bytes 7740288 | tf_op jit(solution)/shard_map/while/body/eval_jaxpr/ko,kgzp->ogzp/dot_general | solution.py:58
  43.2 4.6 %copy.65 = f32[32,4,4096]{0,2,1:T(8,128)} copy(f32[32,4,4096]{2,0,1:T(8,128)S(1)} %get-tuple-element.225) | data formatting | bytes 4194304 | tf_op jit(solution)/shard_map/while/body/eval_jaxpr/jit(silu)/mul | solution.py:103
  47.9 9.5 %reduce_sum.54 = f32[32,2,64,16]{0,3,2,1:T(8,128)S(1)} reduce(f32[32,2,2,64,2,16,2]{0,6,5,4,3,2,1:T(2,128)} %bitcast.123, f32[]{:T(128)} %constant.224.clone.1), dimensions={2,4,6}, to_apply=%region_0.1 | reduce | flops 458752 | bytes 2359300 | tf_op jit(solution)/shard_map/while/body/eval_jaxpr/reduce_sum | solution.py:72
  57.7 4.2 %collective-permute-start.2 = (bf16[32,1,1,1024]{3,0,2,1:T(8,128)(2,1)S(1)}, bf16[32,1,1,1024]{3,0,2,1:T(8,128)(2,1)S(1)}, u32[]{:S(2)}, u32[]{:S(2)}) collective-permute-start(bf16[32,1,1,1024]{3,0,2,1:T(8,128)(2,1)S(1)} %get-tuple-element.219), channel_id=1, source_target_pairs={{0,1},{1,2},{2,3},{3,4},{4,5},{5,6},{6,7},{8,9},{9,10},{10,11},{11... | collective-permute-start | bytes 196616 | tf_op jit(solution)/shard_map/ppermute | solution.py:17
  61.9 1.8 collective-permute-start.3
  63.7 3.3 collective-permute-done.3
  69.8 1.7 copy-done
  71.5 0.9 multiply_reduce_fusion
  72.6 0.4 reduce_sum.57
  73.1 1.3 collective-permute-start.5
  74.4 5.4 %collective-permute-start.4 = (bf16[64,1,1,256]{0,3,2,1:T(8,128)(2,1)S(1)}, bf16[64,1,1,256]{0,3,2,1:T(8,128)(2,1)S(1)}, u32[]{:S(2)}, u32[]{:S(2)}) collective-permute-start(bf16[64,1,1,256]{0,3,2,1:T(8,128)(2,1)S(1)} %fusion.106), channel_id=1, source_target_pairs={{0,1},{1,2},{2,3},{3,4},{4,5},{5,6},{6,7},{8,9},{9,10},{10,11},{11... | collective-permute-start | bytes 98312 | tf_op jit(solution)/shard_map/ppermute | solution.py:17
  79.8 0.7 copy.75
  80.9 6.6 %copy.74 = bf16[108,4096,4]{1,2,0:T(4,128)(2,1)} copy(bf16[108,4096,4]{1,0,2:T(8,128)(2,1)} %bitcast.125) | data formatting | bytes 7077888 | tf_op jit(solution)/shard_map/while/body/eval_jaxpr/kgzp,ogzp->ko/dot_general | solution.py:62
  87.6 0.8 slice_multiply_fusion.72
  88.5 3.4 concatenate.68
  91.8 0.6 copy.83
  92.5 1.4 convert_reduce_fusion.2
  93.9 1.3 collective-permute-start.7
  95.2 5.2 %collective-permute-start.6 = (bf16[128,1,1,256]{0,3,2,1:T(8,128)(2,1)S(1)}, bf16[128,1,1,256]{0,3,2,1:T(8,128)(2,1)S(1)}, u32[]{:S(2)}, u32[]{:S(2)}) collective-permute-start(bf16[128,1,1,256]{0,3,2,1:T(8,128)(2,1)S(1)} %get-tuple-element.156), channel_id=1, source_target_pairs={{0,1},{1,2},{2,3},{3,4},{4,5},{5,6},{6,7},{8,9},{9,10},{10,11},{11... | collective-permute-start | bytes 196616 | tf_op jit(solution)/shard_map/ppermute | solution.py:17
  100.4 1.3 fusion.107
  101.8 0.7 copy.85
  105.1 0.7 fusion.53
  106.6 4.6 %collective-permute-start.8 = (bf16[64,1,1,1024]{3,0,2,1:T(8,128)(2,1)S(1)}, bf16[64,1,1,1024]{3,0,2,1:T(8,128)(2,1)S(1)}, u32[]{:S(2)}, u32[]{:S(2)}) collective-permute-start(bf16[64,1,1,1024]{3,0,2,1:T(8,128)(2,1)S(1)} %get-tuple-element.165), channel_id=1, source_target_pairs={{0,1},{1,2},{2,3},{3,4},{4,5},{5,6},{6,7},{8,9},{9,10},{10,11},{11... | collective-permute-start | bytes 393224 | tf_op jit(solution)/shard_map/ppermute | solution.py:17
  111.1 1.5 collective-permute-start.9
  112.6 3.8 convolution_bitcast_fusion
  116.5 1.6 collective-permute-done.9
  121.8 1.3 fusion.35
  123.5 7.5 %broadcast_in_dim.14 = f32[32,2,2,64,2,16,2]{0,6,5,4,3,2,1:T(2,128)} broadcast(f32[32,2,64,16]{0,3,2,1:T(8,128)S(1)} %bitcast.130), dimensions={0,1,3,5} | broadcast | bytes 2359296 | tf_op jit(solution)/shard_map/broadcast_in_dim | solution.py:79
  131.0 5.3 %copy.81 = f32[32,4,4096]{2,0,1:T(8,128)S(1)} copy(f32[32,4,4096]{0,2,1:T(8,128)} %bitcast.124) | data formatting | bytes 4194304 | tf_op jit(solution)/shard_map/mul | solution.py:82
  136.4 2.7 convert_reduce_fusion
  139.1 3.9 fusion.41
  143.0 85.7 %all-reduce.5 = (f32[27,4,32]{2,0,1:T(8,128)S(1)}, f32[32]{0:T(128)}, f32[64]{0:T(128)}, f32[128]{0:T(128)}) all-reduce(f32[27,4,32]{2,0,1:T(8,128)S(1)} %fusion.41, f32[32]{0:T(128)S(1)} %get-tuple-element.159, f32[64]{0:T(128)S(1)} %get-tuple-element.157, ...), channel_id=1, replica_groups=mesh['sample'=32,'slab'=8] {'sample','slab'}, use_global_device_ids=true, to_apply=%region_3.4 | all-reduce | flops 3680 | bytes 29440 | tf_op jit(solution)/shard_map/psum | solution.py:186
  228.6 0.7 copy.86
  229.3 155.3 %all-reduce.9.cloned.1.call-done = (f32[27,32,64]{2,1,0:T(8,128)}, f32[27,64,128]{2,1,0:T(8,128)}) async-done(((f32[27,32,64]{2,1,0:T(8,128)}, f32[27,64,128]{2,1,0:T(8,128)}), (f32[27,32,64]{2,1,0:T(8,128)}, f32[27,64,128]{2,1,0:T(8,128)})) %all-reduce.9.cloned.1.call-update) | async-done | bytes 1105936 | tf_op jit(solution)/shard_map/psum | solution.py:186
  384.6 1.8 copy.184
  386.4 2.2 copy.185
  (136 shorter events, 10.9 us)
Async XLA Ops:
  7.2 377.4 %all-reduce.9.cloned.1.call-start = ((), (), s32[]{:S(2)}) async-start(), calls=%async_computation | async-start | bytes 2654208 | tf_op jit(solution)/shard_map/psum | solution.py:186
  8.3 9.7 %collective-permute-start = (bf16[4,1,1,4096]{3,0,2,1:T(4,128)(2,1)S(1)}, bf16[4,1,1,4096]{3,0,2,1:T(4,128)(2,1)S(1)}, u32[]{:S(2)}, u32[]{:S(2)}) collective-permute-start(bf16[4,1,1,4096]{3,0,2,1:T(4,128)(2,1)S(1)} %get-tuple-element.223), channel_id=1, source_target_pairs={{0,1},{1,2},{2,3},{3,4},{4,5},{5,6},{6,7},{8,9},{9,10},{10,11},{11... | collective-permute-start | bytes 98312 | tf_op jit(solution)/shard_map/ppermute | solution.py:17
  12.6 5.3 %collective-permute-start.1 = (bf16[4,1,1,4096]{3,0,2,1:T(4,128)(2,1)S(1)}, bf16[4,1,1,4096]{3,0,2,1:T(4,128)(2,1)S(1)}, u32[]{:S(2)}, u32[]{:S(2)}) collective-permute-start(bf16[4,1,1,4096]{3,0,2,1:T(4,128)(2,1)S(1)} %get-tuple-element.224), channel_id=1, source_target_pairs={{1,0},{2,1},{3,2},{4,3},{5,4},{6,5},{7,6},{9,8},{10,9},{11,10},{12... | collective-permute-start | bytes 98312 | tf_op jit(solution)/shard_map/ppermute | solution.py:18
  18.0 2.7 copy-start.8
  18.0 0.6 copy-start.3
  18.6 0.6 copy-start.5
  19.4 1.3 copy-start.4
  19.4 1.3 copy-start.6
  57.7 6.0 %collective-permute-start.2 = (bf16[32,1,1,1024]{3,0,2,1:T(8,128)(2,1)S(1)}, bf16[32,1,1,1024]{3,0,2,1:T(8,128)(2,1)S(1)}, u32[]{:S(2)}, u32[]{:S(2)}) collective-permute-start(bf16[32,1,1,1024]{3,0,2,1:T(8,128)(2,1)S(1)} %get-tuple-element.219), channel_id=1, source_target_pairs={{0,1},{1,2},{2,3},{3,4},{4,5},{5,6},{6,7},{8,9},{9,10},{10,11},{11... | collective-permute-start | bytes 196616 | tf_op jit(solution)/shard_map/ppermute | solution.py:17
  61.9 5.2 %collective-permute-start.3 = (bf16[32,1,1,1024]{3,0,2,1:T(8,128)(2,1)S(1)}, bf16[32,1,1,1024]{3,0,2,1:T(8,128)(2,1)S(1)}, u32[]{:S(2)}, u32[]{:S(2)}) collective-permute-start(bf16[32,1,1,1024]{3,0,2,1:T(8,128)(2,1)S(1)} %get-tuple-element.220), channel_id=1, source_target_pairs={{1,0},{2,1},{3,2},{4,3},{5,4},{6,5},{7,6},{9,8},{10,9},{11,10},{12... | collective-permute-start | bytes 196616 | tf_op jit(solution)/shard_map/ppermute | solution.py:18
  67.3 4.2 %copy-start.2 = (bf16[27,32,64]{2,1,0:T(8,128)(2,1)S(1)}, bf16[27,32,64]{2,1,0:T(8,128)(2,1)}, u32[]{:S(2)}) copy-start(bf16[27,32,64]{2,1,0:T(8,128)(2,1)} %param.12) | copy-start | bytes 331780
  67.3 4.2 %copy-start.9 = (f32[64]{0:T(128)S(1)}, f32[64]{0:T(128)}, u32[]{:S(2)}) copy-start(f32[64]{0:T(128)} %param.13) | copy-start | bytes 772
  69.8 1.7 copy-start
  71.5 8.3 %copy-start.7 = (bf16[128,1,1,256]{3,0,2,1:T(8,128)(2,1)S(1)}, bf16[128,1,1,256]{3,0,2,1:T(8,128)(2,1)}, u32[]{:S(2)}) copy-start(bf16[128,1,1,256]{3,0,2,1:T(8,128)(2,1)} %param.9) | copy-start | bytes 196612
  73.1 14.4 %collective-permute-start.5 = (bf16[64,1,1,256]{0,3,2,1:T(8,128)(2,1)S(1)}, bf16[64,1,1,256]{0,3,2,1:T(8,128)(2,1)S(1)}, u32[]{:S(2)}, u32[]{:S(2)}) collective-permute-start(bf16[64,1,1,256]{0,3,2,1:T(8,128)(2,1)S(1)} %fusion.106), channel_id=1, source_target_pairs={{1,0},{2,1},{3,2},{4,3},{5,4},{6,5},{7,6},{9,8},{10,9},{11,10},{12... | collective-permute-start | bytes 98312 | tf_op jit(solution)/shard_map/ppermute | solution.py:18
  74.4 13.1 %collective-permute-start.4 = (bf16[64,1,1,256]{0,3,2,1:T(8,128)(2,1)S(1)}, bf16[64,1,1,256]{0,3,2,1:T(8,128)(2,1)S(1)}, u32[]{:S(2)}, u32[]{:S(2)}) collective-permute-start(bf16[64,1,1,256]{0,3,2,1:T(8,128)(2,1)S(1)} %fusion.106), channel_id=1, source_target_pairs={{0,1},{1,2},{2,3},{3,4},{4,5},{5,6},{6,7},{8,9},{9,10},{10,11},{11... | collective-permute-start | bytes 98312 | tf_op jit(solution)/shard_map/ppermute | solution.py:17
  87.6 4.9 %copy-start.10 = (f32[128]{0:T(128)S(1)}, f32[128]{0:T(128)}, u32[]{:S(2)}) copy-start(f32[128]{0:T(128)} %param.15) | copy-start | bytes 1540
  93.9 8.6 %collective-permute-start.7 = (bf16[128,1,1,256]{0,3,2,1:T(8,128)(2,1)S(1)}, bf16[128,1,1,256]{0,3,2,1:T(8,128)(2,1)S(1)}, u32[]{:S(2)}, u32[]{:S(2)}) collective-permute-start(bf16[128,1,1,256]{0,3,2,1:T(8,128)(2,1)S(1)} %get-tuple-element.156), channel_id=1, source_target_pairs={{1,0},{2,1},{3,2},{4,3},{5,4},{6,5},{7,6},{9,8},{10,9},{11,10},{12... | collective-permute-start | bytes 196616 | tf_op jit(solution)/shard_map/ppermute | solution.py:18
  95.2 7.3 %collective-permute-start.6 = (bf16[128,1,1,256]{0,3,2,1:T(8,128)(2,1)S(1)}, bf16[128,1,1,256]{0,3,2,1:T(8,128)(2,1)S(1)}, u32[]{:S(2)}, u32[]{:S(2)}) collective-permute-start(bf16[128,1,1,256]{0,3,2,1:T(8,128)(2,1)S(1)} %get-tuple-element.156), channel_id=1, source_target_pairs={{0,1},{1,2},{2,3},{3,4},{4,5},{5,6},{6,7},{8,9},{9,10},{10,11},{11... | collective-permute-start | bytes 196616 | tf_op jit(solution)/shard_map/ppermute | solution.py:17
  106.6 9.9 %collective-permute-start.8 = (bf16[64,1,1,1024]{3,0,2,1:T(8,128)(2,1)S(1)}, bf16[64,1,1,1024]{3,0,2,1:T(8,128)(2,1)S(1)}, u32[]{:S(2)}, u32[]{:S(2)}) collective-permute-start(bf16[64,1,1,1024]{3,0,2,1:T(8,128)(2,1)S(1)} %get-tuple-element.165), channel_id=1, source_target_pairs={{0,1},{1,2},{2,3},{3,4},{4,5},{5,6},{6,7},{8,9},{9,10},{10,11},{11... | collective-permute-start | bytes 393224 | tf_op jit(solution)/shard_map/ppermute | solution.py:17
  111.1 6.9 %collective-permute-start.9 = (bf16[64,1,1,1024]{3,0,2,1:T(8,128)(2,1)S(1)}, bf16[64,1,1,1024]{3,0,2,1:T(8,128)(2,1)S(1)}, u32[]{:S(2)}, u32[]{:S(2)}) collective-permute-start(bf16[64,1,1,1024]{3,0,2,1:T(8,128)(2,1)S(1)} %get-tuple-element.166), channel_id=1, source_target_pairs={{1,0},{2,1},{3,2},{4,3},{5,4},{6,5},{7,6},{9,8},{10,9},{11,10},{12... | collective-permute-start | bytes 393224 | tf_op jit(solution)/shard_map/ppermute | solution.py:18
  136.3 2.7 copy-start.1
Sparse Core Ops, SparseCore 0:
  116.6 267.9 all-reduce.8
where the time goes:
time: 400 us; the launch traced here: 396 us
  waiting for transfers between devices  160 us (40%)
  blocking collectives  85.7 us (21%)
  local copies, waits for them, and re-layouts  61 us (15%)
  starting transfers between devices  30.9 us (8%)
  other arithmetic  24.5 us (6%)
  matrix products  18 us (4%)
  between operations  15.3 us (4%)
    psum x1, waiting for transfers between devices, per_device(): lax.psum((kernel_first, bias_first, kernel_second, bias_second), ('sample...  155 us
    psum x1, blocking collectives, per_device(): lax.psum((kernel_first, bias_first, kernel_second, bias_second), ('sample...  85.7 us
    ppermute x5, starting transfers between devices, with_halo(): before = lax.ppermute(last, axis, up)  23.7 us
    concatenate x3, local copies, waits for them, and re-layouts, gather_taps(): return jnp.concatenate(pieces, axis=0)  20.2 us
    unnamed x52, local copies, waits for them, and re-layouts  12.9 us
    reduce_sum x2, other arithmetic, pool_cells(): grouped.mean(axis=(3, 5, 7))  9.96 us
    dot_general x3, matrix products, weight_term(): jnp.einsum('kgzp,ogzp->ko', patches, grad_block, preferred_element_type=j...  9.02 us
    dot_general x5, matrix products, apply_weight(): jnp.einsum('ko,kgzp->ogzp', flat_weight, patches, preferred_element_type=...  8.99 us
  transfers between devices with their start and end apart: 11, of which 3 were waited for; matrix products, arithmetic and copies ran while one was open for 11% of the time, Pallas kernels for 0%

commit v1 on v0

--- a/solution.py
+++ b/solution.py
@@ -5,6 +5,7 @@
 
 SX = 32
 CZ = 4
+search_the_halves = lambda frame_in: lax.psum(lax.psum(frame_in, "sample"), "slab")
 
 
 def with_halo(shard, sides, width):
@@ -183,8 +184,8 @@
     ).astype(jnp.bfloat16)
     kernel_first = weight_grads(volume_padded, first_delta, SX, CZ, w_first)
     bias_first = bias_sum(first_delta)
-    kernel_first, bias_first, kernel_second, bias_second = lax.psum(
-        (kernel_first, bias_first, kernel_second, bias_second), ("sample", "slab")
+    kernel_first, bias_first, kernel_second, bias_second = search_the_halves(
+        (kernel_first, bias_first, kernel_second, bias_second)
     )
     return (
         features,

time: 400 us -> 581 us (1.45)
  blocking collectives: 85.7 us -> 220 us
  waiting for transfers between devices: 160 us -> 207 us
    psum x1 -> x3, blocking collectives: 85.7 us -> 220 us  [the longest x1 120 us: lax.psum(frame_in, 'sample')]
    psum x1 -> x3, waiting for transfers between devices: 155 us -> 204 us  [the longest x1 117 us: lax.psum(frame_in, 'sample')]
  transfers between devices with their start and end apart: 11 -> 13, of which waited for: 3 -> 3; matrix products, arithmetic and copies ran while one was open for 11% -> 7% of each run, Pallas kernels for 0% -> 0%
where the time goes in v1:
time: 581 us; the launch traced here: 577 us
  blocking collectives  220 us (38%)
  waiting for transfers between devices  207 us (36%)
  local copies, waits for them, and re-layouts  61.2 us (11%)
  starting transfers between devices  30.8 us (5%)
  other arithmetic  24.5 us (4%)
  matrix products  18 us (3%)
  between operations  15 us (3%)
    psum x1, blocking collectives, lax.psum(frame_in, 'sample')  120 us
    psum x1, waiting for transfers between devices, lax.psum(frame_in, 'sample')  117 us
    psum x1, waiting for transfers between devices, per_device(): lax.psum((kernel_third, bias_third), ('sample', 'slab'))  86.8 us
    psum x1, blocking collectives, per_device(): lax.psum((kernel_third, bias_third), ('sample', 'slab'))  77.1 us
    ppermute x5, starting transfers between devices, with_halo(): before = lax.ppermute(last, axis, up)  23.7 us
    psum x1, blocking collectives, lax.psum(lax.psum(frame_in, 'sample'), 'slab')  23 us
    concatenate x3, local copies, waits for them, and re-layouts, gather_taps(): return jnp.concatenate(pieces, axis=0)  20.3 us
    unnamed x52, local copies, waits for them, and re-layouts  12.9 us
  transfers between devices with their start and end apart: 13, of which 3 were waited for; matrix products, arithmetic and copies ran while one was open for 7% of the time, Pallas kernels for 0%

profile of v1, /device:TPU:1, one launch (start us, length us, event | category | flops | bytes accessed | tf_op | source)
XLA Modules:
  0.0 576.9 jit_solution(14404217917900565659)
XLA Ops:
  7.2 1.0 copy.58
  8.3 4.4 collective-permute-start
  12.6 1.3 collective-permute-start.1
  14.6 0.9 reverse_bitcast_fusion.1
  15.5 1.0 reverse_bitcast_fusion
  16.6 1.4 reshape.324
  18.0 0.6 copy-done.3
  18.6 0.6 copy-done.5
  19.4 1.3 slice_multiply_fusion.36
  20.7 1.7 slice_multiply_fusion.37
  22.4 16.3 %concatenate.62 = bf16[108,1,4,4096]{3,0,2,1:T(8,128)(2,1)} concatenate(bf16[4,1,4,4096]{3,0,2,1:T(4,128)(2,1)} %get-tuple-element.212, bf16[4,1,4,4096]{3,0,2,1:T(4,128)(2,1)S(1)} %get-tuple-element.218, bf16[4,1,4,4096]{3,0,2,1:T(4,128)(2,1)S(1)} %get-tuple-element.203, bf16[4,1,4,4096]{3,0,2,1:T(4,128)(2,1)} %get-tuple-element.211, ...), dimensions={0} | concatenate | bytes 7077888 | tf_op jit(solution)/shard_map/while/body/eval_jaxpr/concatenate | solution.py:54
  38.7 4.7 fusion.10
  43.3 4.7 copy.65
  48.0 9.5 %reduce_sum.54 = f32[32,2,64,16]{0,3,2,1:T(8,128)S(1)} reduce(f32[32,2,2,64,2,16,2]{0,6,5,4,3,2,1:T(2,128)} %bitcast.123, f32[]{:T(128)} %constant.224.clone.1), dimensions={2,4,6}, to_apply=%region_0.1 | reduce | flops 458752 | bytes 2359300 | tf_op jit(solution)/shard_map/while/body/eval_jaxpr/reduce_sum | solution.py:73
  57.8 4.2 collective-permute-start.2
  62.0 1.8 collective-permute-start.3
  63.9 3.3 collective-permute-done.3
  69.9 1.7 copy-done
  71.7 0.9 multiply_reduce_fusion
  73.2 1.3 collective-permute-start.5
  74.5 5.4 collective-permute-start.4
  79.9 0.7 copy.75
  81.0 6.6 %copy.74 = bf16[108,4096,4]{1,2,0:T(4,128)(2,1)} copy(bf16[108,4096,4]{1,0,2:T(8,128)(2,1)} %bitcast.125) | data formatting | bytes 7077888 | tf_op jit(solution)/shard_map/while/body/eval_jaxpr/kgzp,ogzp->ko/dot_general | solution.py:63
  87.8 0.8 slice_multiply_fusion.72
  88.6 3.4 concatenate.68
  92.0 0.6 copy.83
  92.7 1.4 convert_reduce_fusion.2
  94.1 1.3 collective-permute-start.7
  95.4 5.2 collective-permute-start.6
  100.6 1.3 fusion.107
  104.5 0.7 fusion.53
  105.9 3.8 convolution_bitcast_fusion
  109.9 4.6 collective-permute-start.8
  114.4 1.3 collective-permute-start.9
  115.7 117.2 %all-reduce.11.cloned.1.call-done = f32[27,32,64]{2,1,0:T(8,128)} async-done(((f32[27,32,64]{2,1,0:T(8,128)}), f32[27,32,64]{2,1,0:T(8,128)}) %all-reduce.11.cloned.1.call-update) | async-done | bytes 221200 | tf_op jit(solution)/shard_map/psum | solution.py:8
  233.0 0.7 copy.85
  233.8 77.1 %psum.79 = f32[128]{0:T(128)} all-reduce(f32[128]{0:T(128)S(1)} %get-tuple-element.150), channel_id=1, replica_groups=mesh['sample'=32,'slab'=8] {'sample','slab'}, use_global_device_ids=true, to_apply=%region_15.16 | all-reduce | flops 128 | bytes 1024 | tf_op jit(solution)/shard_map/psum | solution.py:170
  314.7 1.3 fusion.35
  316.4 7.6 %broadcast_in_dim.14 = f32[32,2,2,64,2,16,2]{0,6,5,4,3,2,1:T(2,128)} broadcast(f32[32,2,64,16]{0,3,2,1:T(8,128)S(1)} %bitcast.130), dimensions={0,1,3,5} | broadcast | bytes 2359296 | tf_op jit(solution)/shard_map/broadcast_in_dim | solution.py:80
  323.9 5.3 copy.81
  329.3 2.7 convert_reduce_fusion
  332.0 3.9 fusion.41
  335.9 119.9 %all-reduce.5 = (f32[27,4,32]{2,0,1:T(8,128)S(1)}, f32[32]{0:T(128)S(1)}, f32[64]{0:T(128)S(1)}) all-reduce(f32[27,4,32]{2,0,1:T(8,128)S(1)} %fusion.41, f32[32]{0:T(128)S(1)} %get-tuple-element.159, f32[64]{0:T(128)S(1)} %get-tuple-element.157), channel_id=1, replica_groups=mesh['sample'=32,'slab'=8] {'sample'}, use_global_device_ids=true, to_apply=%region_3.4 | all-reduce | flops 3552 | bytes 28416 | tf_op jit(solution)/shard_map/psum | solution.py:8
  455.8 23.0 %all-reduce.6 = (f32[27,4,32]{2,0,1:T(8,128)S(1)}, f32[32]{0:T(128)}, f32[64]{0:T(128)}) all-reduce(f32[27,4,32]{2,0,1:T(8,128)S(1)} %get-tuple-element.139, f32[32]{0:T(128)S(1)} %get-tuple-element.140, f32[64]{0:T(128)S(1)} %get-tuple-element.146), channel_id=1, replica_groups=mesh['sample'=32,'slab'=8] {'slab'}, use_global_device_ids=true, to_apply=%region_4.5 | all-reduce | flops 3552 | bytes 28416 | tf_op jit(solution)/shard_map/psum | solution.py:8
  478.8 0.7 copy.86
  479.5 86.8 %all-reduce.15.cloned.1.call-done = f32[27,64,128]{2,1,0:T(8,128)} async-done(((f32[27,64,128]{2,1,0:T(8,128)}), f32[27,64,128]{2,1,0:T(8,128)}) %all-reduce.15.cloned.1.call-update) | async-done | bytes 884752 | tf_op jit(solution)/shard_map/psum | solution.py:170
  566.2 1.8 copy.185
  568.0 2.2 copy.186
  (144 shorter events, 12.1 us)
Async XLA Ops:
  7.2 225.7 %all-reduce.11.cloned.1.call-start = ((), (), s32[]{:S(2)}) async-start(), calls=%async_computation | async-start | bytes 884736 | tf_op jit(solution)/shard_map/psum | solution.py:8
  8.3 9.7 %collective-permute-start = (bf16[4,1,1,4096]{3,0,2,1:T(4,128)(2,1)S(1)}, bf16[4,1,1,4096]{3,0,2,1:T(4,128)(2,1)S(1)}, u32[]{:S(2)}, u32[]{:S(2)}) collective-permute-start(bf16[4,1,1,4096]{3,0,2,1:T(4,128)(2,1)S(1)} %get-tuple-element.223), channel_id=1, source_target_pairs={{0,1},{1,2},{2,3},{3,4},{4,5},{5,6},{6,7},{8,9},{9,10},{10,11},{11... | collective-permute-start | bytes 98312 | tf_op jit(solution)/shard_map/ppermute | solution.py:18
  12.6 5.3 collective-permute-start.1
  18.0 2.7 copy-start.8
  18.0 0.6 copy-start.3
  18.6 0.6 copy-start.5
  19.4 1.3 copy-start.4
  19.4 1.3 copy-start.6
  57.8 6.0 %collective-permute-start.2 = (bf16[32,1,1,1024]{3,0,2,1:T(8,128)(2,1)S(1)}, bf16[32,1,1,1024]{3,0,2,1:T(8,128)(2,1)S(1)}, u32[]{:S(2)}, u32[]{:S(2)}) collective-permute-start(bf16[32,1,1,1024]{3,0,2,1:T(8,128)(2,1)S(1)} %get-tuple-element.219), channel_id=1, source_target_pairs={{0,1},{1,2},{2,3},{3,4},{4,5},{5,6},{6,7},{8,9},{9,10},{10,11},{11... | collective-permute-start | bytes 196616 | tf_op jit(solution)/shard_map/ppermute | solution.py:18
  62.0 5.2 collective-permute-start.3
  67.4 4.3 copy-start.2
  67.4 4.2 copy-start.9
  69.9 1.8 copy-start
  71.7 8.2 %copy-start.7 = (bf16[128,1,1,256]{3,0,2,1:T(8,128)(2,1)S(1)}, bf16[128,1,1,256]{3,0,2,1:T(8,128)(2,1)}, u32[]{:S(2)}) copy-start(bf16[128,1,1,256]{3,0,2,1:T(8,128)(2,1)} %param.9) | copy-start | bytes 196612
  73.2 14.4 %collective-permute-start.5 = (bf16[64,1,1,256]{0,3,2,1:T(8,128)(2,1)S(1)}, bf16[64,1,1,256]{0,3,2,1:T(8,128)(2,1)S(1)}, u32[]{:S(2)}, u32[]{:S(2)}) collective-permute-start(bf16[64,1,1,256]{0,3,2,1:T(8,128)(2,1)S(1)} %fusion.106), channel_id=1, source_target_pairs={{1,0},{2,1},{3,2},{4,3},{5,4},{6,5},{7,6},{9,8},{10,9},{11,10},{12... | collective-permute-start | bytes 98312 | tf_op jit(solution)/shard_map/ppermute | solution.py:19
  74.5 13.1 %collective-permute-start.4 = (bf16[64,1,1,256]{0,3,2,1:T(8,128)(2,1)S(1)}, bf16[64,1,1,256]{0,3,2,1:T(8,128)(2,1)S(1)}, u32[]{:S(2)}, u32[]{:S(2)}) collective-permute-start(bf16[64,1,1,256]{0,3,2,1:T(8,128)(2,1)S(1)} %fusion.106), channel_id=1, source_target_pairs={{0,1},{1,2},{2,3},{3,4},{4,5},{5,6},{6,7},{8,9},{9,10},{10,11},{11... | collective-permute-start | bytes 98312 | tf_op jit(solution)/shard_map/ppermute | solution.py:18
  87.8 4.9 copy-start.10
  94.1 7.8 %collective-permute-start.7 = (bf16[128,1,1,256]{0,3,2,1:T(8,128)(2,1)S(1)}, bf16[128,1,1,256]{0,3,2,1:T(8,128)(2,1)S(1)}, u32[]{:S(2)}, u32[]{:S(2)}) collective-permute-start(bf16[128,1,1,256]{0,3,2,1:T(8,128)(2,1)S(1)} %get-tuple-element.156), channel_id=1, source_target_pairs={{1,0},{2,1},{3,2},{4,3},{5,4},{6,5},{7,6},{9,8},{10,9},{11,10},{12... | collective-permute-start | bytes 196616 | tf_op jit(solution)/shard_map/ppermute | solution.py:19
  95.4 6.5 %collective-permute-start.6 = (bf16[128,1,1,256]{0,3,2,1:T(8,128)(2,1)S(1)}, bf16[128,1,1,256]{0,3,2,1:T(8,128)(2,1)S(1)}, u32[]{:S(2)}, u32[]{:S(2)}) collective-permute-start(bf16[128,1,1,256]{0,3,2,1:T(8,128)(2,1)S(1)} %get-tuple-element.156), channel_id=1, source_target_pairs={{0,1},{1,2},{2,3},{3,4},{4,5},{5,6},{6,7},{8,9},{9,10},{10,11},{11... | collective-permute-start | bytes 196616 | tf_op jit(solution)/shard_map/ppermute | solution.py:18
  109.8 369.7 %all-reduce.13.cloned.1.call-start = ((), (), s32[]{:S(2)}) async-start(), calls=%async_computation.1 | async-start | bytes 884736 | tf_op jit(solution)/shard_map/psum | solution.py:8
  109.9 201.1 %collective-permute-start.8 = (bf16[64,1,1,1024]{3,0,2,1:T(8,128)(2,1)S(1)}, bf16[64,1,1,1024]{3,0,2,1:T(8,128)(2,1)S(1)}, u32[]{:S(2)}, u32[]{:S(2)}) collective-permute-start(bf16[64,1,1,1024]{3,0,2,1:T(8,128)(2,1)S(1)} %get-tuple-element.165), channel_id=1, source_target_pairs={{0,1},{1,2},{2,3},{3,4},{4,5},{5,6},{6,7},{8,9},{9,10},{10,11},{11... | collective-permute-start | bytes 393224 | tf_op jit(solution)/shard_map/ppermute | solution.py:18
  114.4 196.5 %collective-permute-start.9 = (bf16[64,1,1,1024]{3,0,2,1:T(8,128)(2,1)S(1)}, bf16[64,1,1,1024]{3,0,2,1:T(8,128)(2,1)S(1)}, u32[]{:S(2)}, u32[]{:S(2)}) collective-permute-start(bf16[64,1,1,1024]{3,0,2,1:T(8,128)(2,1)S(1)} %get-tuple-element.166), channel_id=1, source_target_pairs={{1,0},{2,1},{3,2},{4,3},{5,4},{6,5},{7,6},{9,8},{10,9},{11,10},{12... | collective-permute-start | bytes 393224 | tf_op jit(solution)/shard_map/ppermute | solution.py:19
  232.9 333.3 %all-reduce.15.cloned.1.call-start = ((), (), s32[]{:S(2)}) async-start(), calls=%async_computation.2 | async-start | bytes 1769472 | tf_op jit(solution)/shard_map/psum | solution.py:170
  329.3 2.7 copy-start.1
Sparse Core Ops, SparseCore 0:
  109.9 122.9 all-reduce.10
  235.4 67.7 all-reduce.12
  309.2 256.9 all-reduce.14
